TPU v7x, 256 devices: a whole 4x4x8 slice. The times are simulated.
256 devices in a mesh: row: 8 (over z), col: 32 (over y, x, core).
Axes of the slice: x: 4, y: 4, z: 8, core: 2. Of those that a mesh axis runs over, the one named last changes fastest.
Arguments:
- tokens: bfloat16 [512, 8192], P('col', 'row'), may hold values from -6 to 6
- cotangent: bfloat16 [512, 8192], P('col', 'row'), may hold values from -6 to 6
- w_gate: bfloat16 [8192, 16384], P('row', 'col'), may hold values from -0.09375 to 0.09375
- w_up: bfloat16 [8192, 16384], P('row', 'col'), may hold values from -0.09375 to 0.09375
- w_down: bfloat16 [16384, 8192], P('col', 'row'), may hold values from -0.0625 to 0.0625
- order_gate: int32 [2048], replicated, may hold values from 0 to 2047, each once
- order_up: int32 [2048], replicated, may hold values from 0 to 2047, each once
- order_down: int32 [2048], replicated, may hold values from 0 to 2047, each once
Outputs:
- output: bfloat16 [512, 8192], P('col', 'row')
- input_grad: bfloat16 [512, 8192], P('col', 'row')
- gate_weight_grad: float32 [8192, 16384], P('row', 'col')
- up_weight_grad: float32 [8192, 16384], P('row', 'col')
- down_weight_grad: float32 [16384, 8192], P('col', 'row')
Inputs may be any that keep to these rules, and one draw needn't show every extreme that they name: `order_gate`: each of the 2048 block numbers appears exactly once. `order_up`: each of the 2048 block numbers appears exactly once. `order_down`: each of the 2048 block numbers appears exactly once.
All inputs are finite; a program needn't handle non-finite values.
Results may differ from a plain program's by a relative error of at most 0.0049.
Values may be sent and summed in bfloat16 or wider, within the bound.
No kernel may reach another device: no remote copies, remote signals or barrier semaphores. Data moves between devices by JAX's collectives and lax.ppermute only.
A program may use at most 64 MiB of HBM per device.

v0:
```python
import jax
import jax.numpy as jnp
from jax import lax
from jax.sharding import PartitionSpec as P

BLOCK = 256


def kept_table(order, row_first, col_first, row_count, col_count, stride):
    kept_count = order.shape[0] // 2
    row_ids = row_first + jnp.arange(row_count, dtype=jnp.int32)
    col_ids = col_first + jnp.arange(col_count, dtype=jnp.int32)
    block_ids = row_ids[:, None] * stride + col_ids[None, :]
    return jnp.any(block_ids[:, :, None] == order[:kept_count][None, None, :], axis=2)


def expand_mask(kept_mask):
    row_count, col_count = kept_mask.shape
    spread = jnp.broadcast_to(kept_mask[:, None, :, None], (row_count, BLOCK, col_count, BLOCK))
    return spread.reshape(row_count * BLOCK, col_count * BLOCK)


def dense_apply(left_operand, right_operand, kept_mask, product_kind):
    full_mask = expand_mask(kept_mask)
    if product_kind == "forward":
        masked = right_operand * full_mask.astype(right_operand.dtype)
        return jnp.dot(left_operand, masked, preferred_element_type=jnp.float32)
    if product_kind == "transposed":
        masked = right_operand * full_mask.astype(right_operand.dtype)
        return lax.dot_general(
            left_operand, masked, (((1,), (1,)), ((), ())), preferred_element_type=jnp.float32
        )
    product = lax.dot_general(
        left_operand, right_operand, (((0,), (0,)), ((), ())), preferred_element_type=jnp.float32
    )
    return product * full_mask.astype(jnp.float32)


def apply_blocks(left_operand, right_operand, kept_mask, product_kind):
    return dense_apply(left_operand, right_operand, kept_mask, product_kind)


def a2a_scatter_sum(parts, axis_name):
    count = lax.axis_size(axis_name)
    pieces = parts.reshape((count, parts.shape[0] // count) + parts.shape[1:])
    return lax.all_to_all(pieces, axis_name, 0, 0, tiled=True).sum(axis=0)


def a2a_gather(block, axis_name):
    count = lax.axis_size(axis_name)
    spread = jnp.broadcast_to(block[None], (count,) + block.shape)
    gathered = lax.all_to_all(spread, axis_name, 0, 0, tiled=True)
    return gathered.reshape((count * block.shape[0],) + block.shape[1:])


def on_device(tokens, cotangent, w_gate, w_up, w_down, order_gate, order_up, order_down):
    rows_here = w_gate.shape[0] // BLOCK
    cols_here = w_gate.shape[1] // BLOCK
    row_start = lax.axis_index("row") * rows_here
    col_start = lax.axis_index("col") * cols_here
    width_blocks = rows_here * lax.axis_size("row")
    hidden_blocks = cols_here * lax.axis_size("col")
    hidden_here = w_gate.shape[1]
    keep_gate = kept_table(order_gate, row_start, col_start, rows_here, cols_here, hidden_blocks)
    keep_up = kept_table(order_up, row_start, col_start, rows_here, cols_here, hidden_blocks)
    keep_down = kept_table(order_down, col_start, row_start, cols_here, rows_here, width_blocks)
    cotangent_all = lax.all_gather(cotangent, "col", axis=0, tiled=True)
    tokens_all = a2a_gather(tokens, "col")
    gate_term = apply_blocks(tokens_all, w_gate, keep_gate, "forward")
    up_term = apply_blocks(tokens_all, w_up, keep_up, "forward")
    both = a2a_scatter_sum(jnp.concatenate([gate_term, up_term], axis=1), "row")
    gate, up = (both[:, :hidden_here], both[:, hidden_here:])
    hidden_term = apply_blocks(cotangent_all, w_down, keep_down, "transposed")
    hidden_grad = a2a_scatter_sum(hidden_term, "row")
    sigmoid_gate = jax.nn.sigmoid(gate)
    activation = gate * sigmoid_gate
    hidden = (activation * up).astype(jnp.bfloat16)
    hidden_all = a2a_gather(hidden, "row")
    output_term = apply_blocks(hidden_all, w_down, keep_down, "forward")
    output = lax.psum_scatter(output_term, "col", scatter_dimension=0, tiled=True).astype(
        jnp.bfloat16
    )
    gate_grad = (hidden_grad * up * sigmoid_gate * (1.0 + gate * (1.0 - sigmoid_gate))).astype(
        jnp.bfloat16
    )
    up_grad = (hidden_grad * activation).astype(jnp.bfloat16)
    grads_all = a2a_gather(jnp.concatenate([gate_grad, up_grad], axis=1), "row")
    gate_grad_all, up_grad_all = (grads_all[:, :hidden_here], grads_all[:, hidden_here:])
    down_weight_grad = apply_blocks(hidden_all, cotangent_all, keep_down, "weights")
    gate_weight_grad = apply_blocks(tokens_all, gate_grad_all, keep_gate, "weights")
    up_weight_grad = apply_blocks(tokens_all, up_grad_all, keep_up, "weights")
    through_gate = apply_blocks(gate_grad_all, w_gate, keep_gate, "transposed")
    through_up = apply_blocks(up_grad_all, w_up, keep_up, "transposed")
    input_grad = a2a_scatter_sum(through_gate + through_up, "col")
    return (
        output,
        input_grad.astype(jnp.bfloat16),
        gate_weight_grad,
        up_weight_grad,
        down_weight_grad,
    )


def solution(mesh):
    placed = (
        P("col", "row"),
        P("col", "row"),
        P("row", "col"),
        P("row", "col"),
        P("col", "row"),
        P(),
        P(),
        P(),
    )
    return jax.shard_map(
        on_device,
        mesh=mesh,
        in_specs=placed,
        out_specs=(
            P("col", "row"),
            P("col", "row"),
            P("row", "col"),
            P("row", "col"),
            P("col", "row"),
        ),
        check_vma=False,
    )
```

profile of v0, /device:TPU:2, one launch (start us, length us, event | category | flops | bytes accessed | tf_op | source)
XLA Modules:
  0.0 282.0 jit_solution(4696219631229832951)
XLA Ops:
  7.2 0.7 all-gather.2.cloned.1.call-update
  7.9 1.9 broadcast_in_dim.13
  9.8 7.8 %all-to-all-start = ((bf16[32,16,1024]{2,1,0:T(8,128)(2,1)}), bf16[32,16,1024]{2,1,0:T(8,128)(2,1)S(1)}, u32[]{:S(2)}, u32[]{:S(2)}) async-start(bf16[32,16,1024]{2,1,0:T(8,128)(2,1)} %broadcast_in_dim.13), calls=%async_computation | async-start | bytes 2097152 | tf_op jit(solution)/shard_map/all_to_all | solution.py:52
  17.6 0.1 broadcast_add_fusion
  17.6 0.2 compare_reduce_fusion
  17.9 0.3 broadcast_in_dim.16
  18.2 0.3 copy.29
  18.5 44.1 %all-gather.2.cloned.1.call-done = bf16[512,1024]{1,0:T(8,128)(2,1)} async-done(((bf16[16,1024]{1,0:T(8,128)(2,1)}), bf16[512,1024]{1,0:T(8,128)(2,1)}) %all-gather.2.cloned.1.call-update) | async-done | bytes 1048592 | tf_op jit(solution)/shard_map/all_gather | solution.py:67
  62.5 2.9 %fusion = f32[512,512]{0,1:T(8,128)} fusion(bf16[512,1024]{1,0:T(8,128)(2,1)} %all-gather.2.cloned.1.call-done, pred[512,1024]{1,0:T(8,128)(4,1)S(1)} %bitcast.50, bf16[512,1024]{1,0:T(8,128)(2,1)S(1)} %copy-done.13), kind=kOutput, calls=%fused_computation.7 | convolution fusion | flops 537395200 | bytes 3670016 | tf_op jit(solution)/shard_map/dot_general | solution.py:30
  65.5 7.0 %all-to-all-start.3 = ((f32[8,64,512]{2,1,0:T(8,128)}), f32[8,64,512]{2,1,0:T(8,128)S(1)}, u32[]{:S(2)}, u32[]{:S(2)}) async-start(f32[8,64,512]{2,1,0:T(8,128)} %bitcast.57), calls=%async_computation.4 | async-start | bytes 2097152 | tf_op jit(solution)/shard_map/all_to_all | solution.py:46
  72.5 0.1 broadcast_add_fusion.1
  72.6 0.2 compare_reduce_fusion.2
  72.8 0.3 broadcast_in_dim.14
  73.2 0.3 copy.28
  73.5 1.7 copy.23
  75.2 0.3 broadcast_in_dim.12
  75.5 1.1 copy.27
  76.6 2.3 copy.22
  78.8 2.1 convolution_bitcast_fusion
  81.0 0.8 convolution_bitcast_fusion.1
  81.8 0.2 pad_maximum_fusion
  82.0 1.8 copy.24
  83.8 17.9 %all-to-all-done.3 = f32[8,64,512]{2,1,0:T(8,128)S(1)} async-done(((f32[8,64,512]{2,1,0:T(8,128)}), f32[8,64,512]{2,1,0:T(8,128)S(1)}, u32[]{:S(2)}, u32[]{:S(2)}) %all-to-all-start.3) | async-done | bytes 1048608 | tf_op jit(solution)/shard_map/all_to_all | solution.py:46
  101.7 3.6 %all-to-all-start.1 = ((f32[8,64,1024]{2,1,0:T(8,128)}), f32[8,64,1024]{2,1,0:T(8,128)S(1)}, u32[]{:S(2)}, u32[]{:S(2)}) async-start(f32[8,64,1024]{2,1,0:T(8,128)} %bitcast.37), calls=%async_computation.1 | async-start | bytes 4194304 | tf_op jit(solution)/shard_map/all_to_all | solution.py:46
  105.3 0.1 reduce_sum.28
  105.4 51.5 %all-to-all-done.1 = f32[8,64,1024]{2,1,0:T(8,128)S(1)} async-done(((f32[8,64,1024]{2,1,0:T(8,128)}), f32[8,64,1024]{2,1,0:T(8,128)S(1)}, u32[]{:S(2)}, u32[]{:S(2)}) %all-to-all-start.1) | async-done | bytes 2097184 | tf_op jit(solution)/shard_map/all_to_all | solution.py:46
  156.9 0.1 reduce_sum.27
  157.0 0.1 multiply_convert_fusion.1
  157.1 0.8 broadcast_in_dim.15
  158.0 3.6 %all-to-all-start.2 = ((bf16[8,64,512]{2,1,0:T(8,128)(2,1)}), bf16[8,64,512]{2,1,0:T(8,128)(2,1)S(1)}, u32[]{:S(2)}, u32[]{:S(2)}) async-start(bf16[8,64,512]{2,1,0:T(8,128)(2,1)} %broadcast_in_dim.15), calls=%async_computation.2 | async-start | bytes 1048576 | tf_op jit(solution)/shard_map/all_to_all | solution.py:52
  161.6 15.9 %all-to-all-done.2 = bf16[8,64,512]{2,1,0:T(8,128)(2,1)S(1)} async-done(((bf16[8,64,512]{2,1,0:T(8,128)(2,1)}), bf16[8,64,512]{2,1,0:T(8,128)(2,1)S(1)}, u32[]{:S(2)}, u32[]{:S(2)}) %all-to-all-start.2) | async-done | bytes 524320 | tf_op jit(solution)/shard_map/all_to_all | solution.py:52
  177.5 1.1 broadcast_in_dim.17
  178.6 3.6 %all-to-all-start.4 = ((bf16[8,64,1024]{2,1,0:T(8,128)(2,1)}), bf16[8,64,1024]{2,1,0:T(8,128)(2,1)S(1)}, u32[]{:S(2)}, u32[]{:S(2)}) async-start(bf16[8,64,1024]{2,1,0:T(8,128)(2,1)} %broadcast_in_dim.17), calls=%async_computation.5 | async-start | bytes 2097152 | tf_op jit(solution)/shard_map/all_to_all | solution.py:52
  182.2 0.0 reduce-scatter.2.cloned.1.call-start
  182.2 2.0 fusion.2
  184.3 24.2 %all-to-all-done.4 = bf16[8,64,1024]{2,1,0:T(8,128)(2,1)S(1)} async-done(((bf16[8,64,1024]{2,1,0:T(8,128)(2,1)}), bf16[8,64,1024]{2,1,0:T(8,128)(2,1)S(1)}, u32[]{:S(2)}, u32[]{:S(2)}) %all-to-all-start.4) | async-done | bytes 1048608 | tf_op jit(solution)/shard_map/all_to_all | solution.py:52
  208.5 2.4 fusion.6
  210.9 2.1 convolution_add_fusion
  213.0 5.9 %all-to-all-start.5 = ((f32[32,16,1024]{2,1,0:T(8,128)}), f32[32,16,1024]{2,1,0:T(8,128)S(1)}, u32[]{:S(2)}, u32[]{:S(2)}) async-start(f32[32,16,1024]{2,1,0:T(8,128)} %bitcast.8), calls=%async_computation.6 | async-start | bytes 4194304 | tf_op jit(solution)/shard_map/all_to_all | solution.py:46
  218.9 3.4 %convolution_select_fusion = f32[512,1024]{1,0:T(8,128)} fusion(pred[512,1024]{1,0:T(8,128)(4,1)S(1)} %bitcast.52, bf16[512,512]{1,0:T(8,128)(2,1)S(1)} %bitcast.39, bf16[512,1024]{1,0:T(8,128)(2,1)} %all-gather.2.cloned.1.call-done), kind=kOutput, calls=%fused_computation.3 | convolution fusion | flops 537395200 | bytes 4194304 | tf_op jit(solution)/shard_map/dot_general | solution.py:33
  222.3 2.1 bitcast_select_fusion.1
  224.4 3.0 %copy.25 = f32[1024,512]{1,0:T(8,128)} copy(f32[1024,512]{0,1:T(8,128)} %bitcast_select_fusion.1) | data formatting | bytes 4194304
  227.3 3.5 %bitcast_select_fusion = f32[1024,512]{0,1:T(8,128)} fusion(pred[1024,512]{0,1:T(8,128)(4,1)} %bitcast.45, bf16[512,1024]{1,0:T(8,128)(2,1)} %bitcast.54, bf16[512,1024]{1,0:T(8,128)(2,1)S(1)} %bitcast.43), kind=kOutput, calls=%fused_computation.1 | convolution fusion | flops 537395200 | bytes 4194304 | tf_op jit(solution)/shard_map/dot_general | solution.py:33
  230.8 2.9 %copy.26 = f32[1024,512]{1,0:T(8,128)} copy(f32[1024,512]{0,1:T(8,128)} %bitcast_select_fusion) | data formatting | bytes 4194304
  233.7 14.9 %all-to-all-done.5 = f32[32,16,1024]{2,1,0:T(8,128)S(1)} async-done(((f32[32,16,1024]{2,1,0:T(8,128)}), f32[32,16,1024]{2,1,0:T(8,128)S(1)}, u32[]{:S(2)}, u32[]{:S(2)}) %all-to-all-start.5) | async-done | bytes 2097184 | tf_op jit(solution)/shard_map/all_to_all | solution.py:46
  248.6 0.7 reduce_sum.29
  249.3 24.4 %reduce-scatter.2.cloned.1.call-done = f32[16,1024]{1,0:T(8,128)} async-done(((f32[512,1024]{1,0:T(8,128)}), f32[16,1024]{1,0:T(8,128)}) %reduce-scatter.2.cloned.1.call-update) | async-done | bytes 65552 | tf_op jit(solution)/shard_map/reduce_scatter | solution.py:80
  273.7 1.5 convert_element_type.11
  (48 shorter events, 0.2 us)
Async XLA Ops:
  7.2 10.5 %slice-start = ((s32[2048]{0:T(1024)}), s32[1024]{0:T(1024)S(1)}, s32[]{:S(2)}) async-start(s32[2048]{0:T(1024)} %param.15), calls=%async_computation.9 | async-start | bytes 8192 | tf_op jit(solution)/shard_map/slice | solution.py:14
  7.2 55.4 %all-gather.2.cloned.1.call-start = ((), (), s32[]{:S(2)}) async-start(), calls=%async_computation.8 | async-start | bytes 1081344 | tf_op jit(solution)/shard_map/all_gather | solution.py:67
  9.8 52.8 %copy-start.13 = (bf16[512,1024]{1,0:T(8,128)(2,1)S(1)}, bf16[512,1024]{1,0:T(8,128)(2,1)}, u32[]{:S(2)}) copy-start(bf16[512,1024]{1,0:T(8,128)(2,1)} %param.12) | copy-start | bytes 3145732
  9.8 55.7 %all-to-all-start = ((bf16[32,16,1024]{2,1,0:T(8,128)(2,1)}), bf16[32,16,1024]{2,1,0:T(8,128)(2,1)S(1)}, u32[]{:S(2)}, u32[]{:S(2)}) async-start(bf16[32,16,1024]{2,1,0:T(8,128)(2,1)} %broadcast_in_dim.13), calls=%async_computation | async-start | bytes 2097152 | tf_op jit(solution)/shard_map/all_to_all | solution.py:52
  18.5 47.0 %copy-start.7 = (pred[64,8,4,256]{3,1,2,0:T(8,128)(4,1)}, pred[64,8,4,256]{3,1,2,0:T(8,128)(4,1)S(1)}, u32[]{:S(2)}) copy-start(pred[64,8,4,256]{3,1,2,0:T(8,128)(4,1)S(1)} %copy.29) | copy-start | bytes 1572868
  65.5 7.1 %slice-start.1 = ((s32[2048]{0:T(1024)}), s32[1024]{0:T(1024)S(1)}, s32[]{:S(2)}) async-start(s32[2048]{0:T(1024)} %param.13), calls=%async_computation.10 | async-start | bytes 8192 | tf_op jit(solution)/shard_map/slice | solution.py:14
  65.5 7.1 %slice-start.2 = ((s32[2048]{0:T(1024)}), s32[1024]{0:T(1024)S(1)}, s32[]{:S(2)}) async-start(s32[2048]{0:T(1024)} %param.14), calls=%async_computation.11 | async-start | bytes 8192 | tf_op jit(solution)/shard_map/slice | solution.py:14
  65.5 7.7 %copy-start.9 = (bf16[32,16,1024]{2,1,0:T(8,128)(2,1)}, bf16[32,16,1024]{2,1,0:T(8,128)(2,1)S(1)}, u32[]{:S(2)}) copy-start(bf16[32,16,1024]{2,1,0:T(8,128)(2,1)S(1)} %all-to-all-done) | copy-start | bytes 3145732
  65.5 36.2 %all-to-all-start.3 = ((f32[8,64,512]{2,1,0:T(8,128)}), f32[8,64,512]{2,1,0:T(8,128)S(1)}, u32[]{:S(2)}, u32[]{:S(2)}) async-start(f32[8,64,512]{2,1,0:T(8,128)} %bitcast.57), calls=%async_computation.4 | async-start | bytes 2097152 | tf_op jit(solution)/shard_map/all_to_all | solution.py:46
  73.5 7.5 %copy-start.5 = (pred[64,8,4,256]{3,1,2,0:T(8,128)(4,1)}, pred[64,8,4,256]{3,1,2,0:T(8,128)(4,1)S(1)}, u32[]{:S(2)}) copy-start(pred[64,8,4,256]{3,1,2,0:T(8,128)(4,1)S(1)} %copy.28) | copy-start | bytes 1572868
  75.2 5.8 %copy-start = (bf16[1024,512]{0,1:T(8,128)(2,1)}, bf16[1024,512]{0,1:T(8,128)(2,1)S(1)}, u32[]{:S(2)}) copy-start(bf16[1024,512]{0,1:T(8,128)(2,1)S(1)} %copy.23) | copy-start | bytes 3145732
  78.8 2.1 copy-start.10
  78.8 2.2 copy-start.12
  78.8 2.2 copy-start.15
  101.7 55.2 %all-to-all-start.1 = ((f32[8,64,1024]{2,1,0:T(8,128)}), f32[8,64,1024]{2,1,0:T(8,128)S(1)}, u32[]{:S(2)}, u32[]{:S(2)}) async-start(f32[8,64,1024]{2,1,0:T(8,128)} %bitcast.37), calls=%async_computation.1 | async-start | bytes 4194304 | tf_op jit(solution)/shard_map/all_to_all | solution.py:46
  158.0 24.2 %copy-start.8 = (pred[64,8,4,256]{3,1,2,0:T(8,128)(4,1)S(1)}, pred[64,8,4,256]{3,1,2,0:T(8,128)(4,1)}, u32[]{:S(2)}) copy-start(pred[64,8,4,256]{3,1,2,0:T(8,128)(4,1)} %copy-done.7) | copy-start | bytes 1572868
  158.0 24.2 %copy-start.14 = (bf16[512,1024]{1,0:T(8,128)(2,1)S(1)}, bf16[512,1024]{1,0:T(8,128)(2,1)}, u32[]{:S(2)}) copy-start(bf16[512,1024]{1,0:T(8,128)(2,1)} %param.12) | copy-start | bytes 3145732
  158.0 19.5 %all-to-all-start.2 = ((bf16[8,64,512]{2,1,0:T(8,128)(2,1)}), bf16[8,64,512]{2,1,0:T(8,128)(2,1)S(1)}, u32[]{:S(2)}, u32[]{:S(2)}) async-start(bf16[8,64,512]{2,1,0:T(8,128)(2,1)} %broadcast_in_dim.15), calls=%async_computation.2 | async-start | bytes 1048576 | tf_op jit(solution)/shard_map/all_to_all | solution.py:52
  178.6 29.9 %all-to-all-start.4 = ((bf16[8,64,1024]{2,1,0:T(8,128)(2,1)}), bf16[8,64,1024]{2,1,0:T(8,128)(2,1)S(1)}, u32[]{:S(2)}, u32[]{:S(2)}) async-start(bf16[8,64,1024]{2,1,0:T(8,128)(2,1)} %broadcast_in_dim.17), calls=%async_computation.5 | async-start | bytes 2097152 | tf_op jit(solution)/shard_map/all_to_all | solution.py:52
  182.2 91.5 %reduce-scatter.2.cloned.1.call-start = ((), (), s32[]{:S(2)}) async-start(), calls=%async_computation.7 | async-start | bytes 2162688 | tf_op jit(solution)/shard_map/reduce_scatter | solution.py:80
  184.3 24.2 %copy-start.16 = (pred[64,8,4,256]{3,1,2,0:T(8,128)(4,1)S(1)}, pred[64,8,4,256]{3,1,2,0:T(8,128)(4,1)}, u32[]{:S(2)}) copy-start(pred[64,8,4,256]{3,1,2,0:T(8,128)(4,1)} %copy.27) | copy-start | bytes 1572868
  208.5 2.4 copy-start.2
  208.5 2.4 copy-start.1
  208.5 2.4 copy-start.6
  213.0 35.6 %all-to-all-start.5 = ((f32[32,16,1024]{2,1,0:T(8,128)}), f32[32,16,1024]{2,1,0:T(8,128)S(1)}, u32[]{:S(2)}, u32[]{:S(2)}) async-start(f32[32,16,1024]{2,1,0:T(8,128)} %bitcast.8), calls=%async_computation.6 | async-start | bytes 4194304 | tf_op jit(solution)/shard_map/all_to_all | solution.py:46
  218.8 3.5 %copy-start.3 = (bf16[8,64,1024]{2,1,0:T(8,128)(2,1)S(1)}, bf16[8,64,1024]{2,1,0:T(8,128)(2,1)}, u32[]{:S(2)}) copy-start(bf16[8,64,1024]{2,1,0:T(8,128)(2,1)} %copy-done.2) | copy-start | bytes 3145732
  218.8 3.5 %copy-start.11 = (bf16[32,16,1024]{2,1,0:T(8,128)(2,1)S(1)}, bf16[32,16,1024]{2,1,0:T(8,128)(2,1)}, u32[]{:S(2)}) copy-start(bf16[32,16,1024]{2,1,0:T(8,128)(2,1)} %copy-done.9) | copy-start | bytes 3145732
  218.9 3.5 %copy-start.17 = (pred[64,8,4,256]{3,1,2,0:T(8,128)(4,1)S(1)}, pred[64,8,4,256]{3,1,2,0:T(8,128)(4,1)}, u32[]{:S(2)}) copy-start(pred[64,8,4,256]{3,1,2,0:T(8,128)(4,1)} %copy.27) | copy-start | bytes 1572868
  224.4 3.0 %copy-start.4 = (bf16[8,64,1024]{2,1,0:T(8,128)(2,1)S(1)}, bf16[8,64,1024]{2,1,0:T(8,128)(2,1)}, u32[]{:S(2)}) copy-start(bf16[8,64,1024]{2,1,0:T(8,128)(2,1)} %copy-done.2) | copy-start | bytes 3145732
Sparse Core Ops, SparseCore 0:
  10.5 51.9 all-gather.1
  186.8 86.8 reduce-scatter.1
where the time goes:
time: 283 us; the launch traced here: 282 us
  waiting for transfers between devices  193 us (68%)
  starting transfers between devices  31.5 us (11%)
  matrix products  21.3 us (8%)
  local copies, waits for them, and re-layouts  18.1 us (6%)
  between operations  14.4 us (5%)
  other arithmetic  3.28 us (1%)
    all_to_all x3, waiting for transfers between devices, a2a_scatter_sum(): return lax.all_to_all(pieces, axis_name, 0, 0, tiled=True).sum(axis=0)  84.3 us
    all_gather x1, waiting for transfers between devices, on_device(): cotangent_all = lax.all_gather(cotangent, 'col', axis=0, tiled=True)  44.1 us
    all_to_all x3, waiting for transfers between devices, a2a_gather(): gathered = lax.all_to_all(spread, axis_name, 0, 0, tiled=True)  40.1 us
    reduce_scatter x1, waiting for transfers between devices, on_device(): lax.psum_scatter(output_term, 'col', scatter_dimension=0, tiled=True)  24.4 us
    all_to_all x3, starting transfers between devices, a2a_scatter_sum(): return lax.all_to_all(pieces, axis_name, 0, 0, tiled=True).sum(axis=0)  16.5 us
    all_to_all x3, starting transfers between devices, a2a_gather(): gathered = lax.all_to_all(spread, axis_name, 0, 0, tiled=True)  14.9 us
    unnamed x43, local copies, waits for them, and re-layouts  11.4 us
    dot_general x3, matrix products, dense_apply(): lax.dot_general(left_operand, right_operand, (((0,), (0,)), ((), ())), pr...  8.97 us
  transfers between devices with their start and end apart: 8, of which 7 were waited for; matrix products, arithmetic and copies ran while one was open for 14% of the time, Pallas kernels for 0%

commit v1 on v0

--- a/solution.py
+++ b/solution.py
@@ -1,9 +1,19 @@
+import functools
 import jax
 import jax.numpy as jnp
 from jax import lax
 from jax.sharding import PartitionSpec as P
 
 BLOCK = 256
+
+
+def attach_rings(local_values, array_dim):
+    arr_out = jnp.stack([local_values for _ in range(lax.axis_size("col"))])
+    current_arr = lax.all_to_all(arr_out, axis_name="col", split_axis=0, concat_axis=0)
+    return jnp.concatenate(current_arr, axis=array_dim)
+
+
+guide_halves_in = functools.partial(attach_rings, array_dim=0)
 
 
 def kept_table(order, row_first, col_first, row_count, col_count, stride):
@@ -64,7 +74,7 @@
     keep_gate = kept_table(order_gate, row_start, col_start, rows_here, cols_here, hidden_blocks)
     keep_up = kept_table(order_up, row_start, col_start, rows_here, cols_here, hidden_blocks)
     keep_down = kept_table(order_down, col_start, row_start, cols_here, rows_here, width_blocks)
-    cotangent_all = lax.all_gather(cotangent, "col", axis=0, tiled=True)
+    cotangent_all = guide_halves_in(cotangent)
     tokens_all = a2a_gather(tokens, "col")
     gate_term = apply_blocks(tokens_all, w_gate, keep_gate, "forward")
     up_term = apply_blocks(tokens_all, w_up, keep_up, "forward")

time: 283 us -> 273 us (0.965)
  waiting for transfers between devices: 193 us -> 162 us
  blocking collectives: 0 us -> 23.4 us
    all_gather x1 -> x0, waiting for transfers between devices: 44.1 us -> none  [on_device(): cotangent_all = lax.all_gather(cotangent, 'col', axis=0, tiled=True)]
    all_to_all x0 -> x1, blocking collectives: none -> 23.4 us  [attach_rings(): lax.all_to_all(arr_out, axis_name='col', split_axis=0, concat_axis=0)]
    all_to_all x3, waiting for transfers between devices: 40.1 us -> 52.7 us  [a2a_gather(): gathered = lax.all_to_all(spread, axis_name, 0, 0, tiled=True)]
    unnamed x43 -> x49, local copies, waits for them, and re-layouts: 11.4 us -> 12 us
  transfers between devices with their start and end apart: 8 -> 7, of which waited for: 7 -> 7; matrix products, arithmetic and copies ran while one was open for 14% -> 13% of each run, Pallas kernels for 0% -> 0%
where the time goes in v1:
time: 273 us; the launch traced here: 272 us
  waiting for transfers between devices  162 us (59%)
  starting transfers between devices  29.6 us (11%)
  blocking collectives  23.4 us (9%)
  matrix products  20.2 us (7%)
  local copies, waits for them, and re-layouts  18.9 us (7%)
  between operations  14.4 us (5%)
  other arithmetic  3.28 us (1%)
    all_to_all x3, waiting for transfers between devices, a2a_scatter_sum(): return lax.all_to_all(pieces, axis_name, 0, 0, tiled=True).sum(axis=0)  85.3 us
    all_to_all x3, waiting for transfers between devices, a2a_gather(): gathered = lax.all_to_all(spread, axis_name, 0, 0, tiled=True)  52.7 us
    reduce_scatter x1, waiting for transfers between devices, on_device(): lax.psum_scatter(output_term, 'col', scatter_dimension=0, tiled=True)  24.4 us
    all_to_all x1, blocking collectives, attach_rings(): lax.all_to_all(arr_out, axis_name='col', split_axis=0, concat_axis=0)  23.4 us
    all_to_all x3, starting transfers between devices, a2a_scatter_sum(): return lax.all_to_all(pieces, axis_name, 0, 0, tiled=True).sum(axis=0)  17.2 us
    all_to_all x3, starting transfers between devices, a2a_gather(): gathered = lax.all_to_all(spread, axis_name, 0, 0, tiled=True)  12.4 us
    unnamed x49, local copies, waits for them, and re-layouts  12 us
    dot_general x3, matrix products, dense_apply(): lax.dot_general(left_operand, right_operand, (((0,), (0,)), ((), ())), pr...  8.94 us
  transfers between devices with their start and end apart: 7, of which 7 were waited for; matrix products, arithmetic and copies ran while one was open for 13% of the time, Pallas kernels for 0%

profile of v1, /device:TPU:2, one launch (start us, length us, event | category | flops | bytes accessed | tf_op | source)
XLA Modules:
  0.0 272.1 jit_solution(6572268745190616335)
XLA Ops:
  7.2 0.9 stack.2
  8.1 23.4 %all_to_all.35 = bf16[32,16,1024]{2,1,0:T(8,128)(2,1)S(1)} all-to-all(bf16[32,16,1024]{2,1,0:T(8,128)(2,1)S(1)} %stack.2), channel_id=1, replica_groups=mesh['row'=8,'col'=32] {'col'}, dimensions={0} | all-to-all | bytes 2097152 | tf_op jit(solution)/shard_map/all_to_all | solution.py:12
  31.5 1.2 broadcast_in_dim.13
  32.7 5.2 %all-to-all-start = ((bf16[32,16,1024]{2,1,0:T(8,128)(2,1)}), bf16[32,16,1024]{2,1,0:T(8,128)(2,1)S(1)}, u32[]{:S(2)}, u32[]{:S(2)}) async-start(bf16[32,16,1024]{2,1,0:T(8,128)(2,1)} %broadcast_in_dim.13), calls=%async_computation | async-start | bytes 2097152 | tf_op jit(solution)/shard_map/all_to_all | solution.py:62
  38.0 0.2 compare_reduce_fusion
  38.2 0.3 broadcast_in_dim.16
  38.5 0.3 copy.29
  38.8 0.8 copy-done.7
  39.6 1.7 fusion
  41.3 12.6 %all-to-all-done = bf16[32,16,1024]{2,1,0:T(8,128)(2,1)S(1)} async-done(((bf16[32,16,1024]{2,1,0:T(8,128)(2,1)}), bf16[32,16,1024]{2,1,0:T(8,128)(2,1)S(1)}, u32[]{:S(2)}, u32[]{:S(2)}) %all-to-all-start) | async-done | bytes 1048608 | tf_op jit(solution)/shard_map/all_to_all | solution.py:62
  54.0 1.0 copy-done.10
  54.9 8.5 %all-to-all-start.4 = ((f32[8,64,512]{2,1,0:T(8,128)}), f32[8,64,512]{2,1,0:T(8,128)S(1)}, u32[]{:S(2)}, u32[]{:S(2)}) async-start(f32[8,64,512]{2,1,0:T(8,128)} %bitcast.60), calls=%async_computation.5 | async-start | bytes 2097152 | tf_op jit(solution)/shard_map/all_to_all | solution.py:56
  63.5 0.2 compare_reduce_fusion.2
  63.7 0.3 broadcast_in_dim.12
  64.1 1.1 copy.27
  65.1 0.3 broadcast_in_dim.14
  65.5 0.3 copy.28
  65.8 1.3 copy.22
  67.1 1.5 copy.23
  68.6 2.4 convolution_bitcast_fusion
  71.0 0.8 convolution_bitcast_fusion.1
  71.8 0.2 pad_maximum_fusion
  72.0 1.8 copy.24
  73.8 18.8 %all-to-all-done.4 = f32[8,64,512]{2,1,0:T(8,128)S(1)} async-done(((f32[8,64,512]{2,1,0:T(8,128)}), f32[8,64,512]{2,1,0:T(8,128)S(1)}, u32[]{:S(2)}, u32[]{:S(2)}) %all-to-all-start.4) | async-done | bytes 1048608 | tf_op jit(solution)/shard_map/all_to_all | solution.py:56
  92.6 3.6 %all-to-all-start.1 = ((f32[8,64,1024]{2,1,0:T(8,128)}), f32[8,64,1024]{2,1,0:T(8,128)S(1)}, u32[]{:S(2)}, u32[]{:S(2)}) async-start(f32[8,64,1024]{2,1,0:T(8,128)} %bitcast.38), calls=%async_computation.1 | async-start | bytes 4194304 | tf_op jit(solution)/shard_map/all_to_all | solution.py:56
  96.2 0.1 reduce_sum.28
  96.3 51.5 %all-to-all-done.1 = f32[8,64,1024]{2,1,0:T(8,128)S(1)} async-done(((f32[8,64,1024]{2,1,0:T(8,128)}), f32[8,64,1024]{2,1,0:T(8,128)S(1)}, u32[]{:S(2)}, u32[]{:S(2)}) %all-to-all-start.1) | async-done | bytes 2097184 | tf_op jit(solution)/shard_map/all_to_all | solution.py:56
  147.8 0.1 reduce_sum.27
  148.0 0.1 multiply_convert_fusion.1
  148.1 0.8 broadcast_in_dim.15
  148.9 3.6 %all-to-all-start.2 = ((bf16[8,64,512]{2,1,0:T(8,128)(2,1)}), bf16[8,64,512]{2,1,0:T(8,128)(2,1)S(1)}, u32[]{:S(2)}, u32[]{:S(2)}) async-start(bf16[8,64,512]{2,1,0:T(8,128)(2,1)} %broadcast_in_dim.15), calls=%async_computation.2 | async-start | bytes 1048576 | tf_op jit(solution)/shard_map/all_to_all | solution.py:62
  152.6 15.9 %all-to-all-done.2 = bf16[8,64,512]{2,1,0:T(8,128)(2,1)S(1)} async-done(((bf16[8,64,512]{2,1,0:T(8,128)(2,1)}), bf16[8,64,512]{2,1,0:T(8,128)(2,1)S(1)}, u32[]{:S(2)}, u32[]{:S(2)}) %all-to-all-start.2) | async-done | bytes 524320 | tf_op jit(solution)/shard_map/all_to_all | solution.py:62
  168.4 1.1 broadcast_in_dim.17
  169.5 3.6 %all-to-all-start.5 = ((bf16[8,64,1024]{2,1,0:T(8,128)(2,1)}), bf16[8,64,1024]{2,1,0:T(8,128)(2,1)S(1)}, u32[]{:S(2)}, u32[]{:S(2)}) async-start(bf16[8,64,1024]{2,1,0:T(8,128)(2,1)} %broadcast_in_dim.17), calls=%async_computation.6 | async-start | bytes 2097152 | tf_op jit(solution)/shard_map/all_to_all | solution.py:62
  173.1 2.1 fusion.2
  175.2 24.2 %all-to-all-done.5 = bf16[8,64,1024]{2,1,0:T(8,128)(2,1)S(1)} async-done(((bf16[8,64,1024]{2,1,0:T(8,128)(2,1)}), bf16[8,64,1024]{2,1,0:T(8,128)(2,1)S(1)}, u32[]{:S(2)}, u32[]{:S(2)}) %all-to-all-start.5) | async-done | bytes 1048608 | tf_op jit(solution)/shard_map/all_to_all | solution.py:62
  199.4 2.4 fusion.6
  201.8 2.0 convolution_add_fusion
  203.8 5.1 %all-to-all-start.6 = ((f32[32,16,1024]{2,1,0:T(8,128)}), f32[32,16,1024]{2,1,0:T(8,128)S(1)}, u32[]{:S(2)}, u32[]{:S(2)}) async-start(f32[32,16,1024]{2,1,0:T(8,128)} %bitcast.9), calls=%async_computation.7 | async-start | bytes 4194304 | tf_op jit(solution)/shard_map/all_to_all | solution.py:56
  209.0 3.4 %convolution_select_fusion = f32[512,1024]{1,0:T(8,128)} fusion(pred[512,1024]{1,0:T(8,128)(4,1)S(1)} %bitcast.53, bf16[512,512]{1,0:T(8,128)(2,1)S(1)} %bitcast.40, bf16[512,1024]{1,0:T(8,128)(2,1)} %bitcast.59), kind=kOutput, calls=%fused_computation.3 | convolution fusion | flops 537395200 | bytes 4194304 | tf_op jit(solution)/shard_map/dot_general | solution.py:43
  212.4 2.1 bitcast_select_fusion.1
  214.5 3.0 %copy.25 = f32[1024,512]{1,0:T(8,128)} copy(f32[1024,512]{0,1:T(8,128)} %bitcast_select_fusion.1) | data formatting | bytes 4194304
  217.5 3.4 %bitcast_select_fusion = f32[1024,512]{0,1:T(8,128)} fusion(pred[1024,512]{0,1:T(8,128)(4,1)} %bitcast.46, bf16[512,1024]{1,0:T(8,128)(2,1)} %bitcast.55, bf16[512,1024]{1,0:T(8,128)(2,1)S(1)} %bitcast.44), kind=kOutput, calls=%fused_computation.1 | convolution fusion | flops 537395200 | bytes 4194304 | tf_op jit(solution)/shard_map/dot_general | solution.py:43
  220.9 2.9 %copy.26 = f32[1024,512]{1,0:T(8,128)} copy(f32[1024,512]{0,1:T(8,128)} %bitcast_select_fusion) | data formatting | bytes 4194304
  223.8 14.9 %all-to-all-done.6 = f32[32,16,1024]{2,1,0:T(8,128)S(1)} async-done(((f32[32,16,1024]{2,1,0:T(8,128)}), f32[32,16,1024]{2,1,0:T(8,128)S(1)}, u32[]{:S(2)}, u32[]{:S(2)}) %all-to-all-start.6) | async-done | bytes 2097184 | tf_op jit(solution)/shard_map/all_to_all | solution.py:56
  238.7 0.7 reduce_sum.29
  239.4 24.4 %reduce-scatter.2.cloned.1.call-done = f32[16,1024]{1,0:T(8,128)} async-done(((f32[512,1024]{1,0:T(8,128)}), f32[16,1024]{1,0:T(8,128)}) %reduce-scatter.2.cloned.1.call-update) | async-done | bytes 65552 | tf_op jit(solution)/shard_map/reduce_scatter | solution.py:90
  263.8 1.5 convert_element_type.11
  (53 shorter events, 0.3 us)
Async XLA Ops:
  7.2 24.3 %copy-start.20 = (bf16[16,1024]{1,0:T(8,128)(2,1)S(1)}, bf16[16,1024]{1,0:T(8,128)(2,1)}, u32[]{:S(2)}) copy-start(bf16[16,1024]{1,0:T(8,128)(2,1)} %param.8) | copy-start | bytes 98308
  31.5 7.3 %copy-start.13 = (bf16[32,16,1024]{2,1,0:T(8,128)(2,1)}, bf16[32,16,1024]{2,1,0:T(8,128)(2,1)S(1)}, u32[]{:S(2)}) copy-start(bf16[32,16,1024]{2,1,0:T(8,128)(2,1)S(1)} %all_to_all.35) | copy-start | bytes 3145732
  31.5 6.5 %slice-start = ((s32[2048]{0:T(1024)}), s32[1024]{0:T(1024)S(1)}, s32[]{:S(2)}) async-start(s32[2048]{0:T(1024)} %param.15), calls=%async_computation.9 | async-start | bytes 8192 | tf_op jit(solution)/shard_map/slice | solution.py:24
  32.7 6.9 %copy-start.15 = (bf16[512,1024]{1,0:T(8,128)(2,1)S(1)}, bf16[512,1024]{1,0:T(8,128)(2,1)}, u32[]{:S(2)}) copy-start(bf16[512,1024]{1,0:T(8,128)(2,1)} %param.12) | copy-start | bytes 3145732
  32.7 21.3 %all-to-all-start = ((bf16[32,16,1024]{2,1,0:T(8,128)(2,1)}), bf16[32,16,1024]{2,1,0:T(8,128)(2,1)S(1)}, u32[]{:S(2)}, u32[]{:S(2)}) async-start(bf16[32,16,1024]{2,1,0:T(8,128)(2,1)} %broadcast_in_dim.13), calls=%async_computation | async-start | bytes 2097152 | tf_op jit(solution)/shard_map/all_to_all | solution.py:62
  38.8 0.8 copy-start.7
  41.3 22.2 %slice-start.1 = ((s32[2048]{0:T(1024)}), s32[1024]{0:T(1024)S(1)}, s32[]{:S(2)}) async-start(s32[2048]{0:T(1024)} %param.13), calls=%async_computation.10 | async-start | bytes 8192 | tf_op jit(solution)/shard_map/slice | solution.py:24
  41.3 22.2 %slice-start.2 = ((s32[2048]{0:T(1024)}), s32[1024]{0:T(1024)S(1)}, s32[]{:S(2)}) async-start(s32[2048]{0:T(1024)} %param.14), calls=%async_computation.11 | async-start | bytes 8192 | tf_op jit(solution)/shard_map/slice | solution.py:24
  54.0 1.0 copy-start.10
  54.9 37.7 %all-to-all-start.4 = ((f32[8,64,512]{2,1,0:T(8,128)}), f32[8,64,512]{2,1,0:T(8,128)S(1)}, u32[]{:S(2)}, u32[]{:S(2)}) async-start(f32[8,64,512]{2,1,0:T(8,128)} %bitcast.60), calls=%async_computation.5 | async-start | bytes 2097152 | tf_op jit(solution)/shard_map/all_to_all | solution.py:56
  63.4 2.3 copy-start.9
  65.7 5.2 %copy-start.5 = (pred[64,8,4,256]{3,1,2,0:T(8,128)(4,1)}, pred[64,8,4,256]{3,1,2,0:T(8,128)(4,1)S(1)}, u32[]{:S(2)}) copy-start(pred[64,8,4,256]{3,1,2,0:T(8,128)(4,1)S(1)} %copy.28) | copy-start | bytes 1572868
  68.6 2.4 copy-start
  68.6 2.4 copy-start.11
  68.6 2.4 copy-start.14
  68.6 2.4 copy-start.17
  92.6 55.2 %all-to-all-start.1 = ((f32[8,64,1024]{2,1,0:T(8,128)}), f32[8,64,1024]{2,1,0:T(8,128)S(1)}, u32[]{:S(2)}, u32[]{:S(2)}) async-start(f32[8,64,1024]{2,1,0:T(8,128)} %bitcast.38), calls=%async_computation.1 | async-start | bytes 4194304 | tf_op jit(solution)/shard_map/all_to_all | solution.py:56
  148.9 24.2 %copy-start.8 = (pred[64,8,4,256]{3,1,2,0:T(8,128)(4,1)S(1)}, pred[64,8,4,256]{3,1,2,0:T(8,128)(4,1)}, u32[]{:S(2)}) copy-start(pred[64,8,4,256]{3,1,2,0:T(8,128)(4,1)} %copy-done.7) | copy-start | bytes 1572868
  148.9 24.2 %copy-start.16 = (bf16[512,1024]{1,0:T(8,128)(2,1)S(1)}, bf16[512,1024]{1,0:T(8,128)(2,1)}, u32[]{:S(2)}) copy-start(bf16[512,1024]{1,0:T(8,128)(2,1)} %param.12) | copy-start | bytes 3145732
  148.9 19.5 %all-to-all-start.2 = ((bf16[8,64,512]{2,1,0:T(8,128)(2,1)}), bf16[8,64,512]{2,1,0:T(8,128)(2,1)S(1)}, u32[]{:S(2)}, u32[]{:S(2)}) async-start(bf16[8,64,512]{2,1,0:T(8,128)(2,1)} %broadcast_in_dim.15), calls=%async_computation.2 | async-start | bytes 1048576 | tf_op jit(solution)/shard_map/all_to_all | solution.py:62
  169.5 29.9 %all-to-all-start.5 = ((bf16[8,64,1024]{2,1,0:T(8,128)(2,1)}), bf16[8,64,1024]{2,1,0:T(8,128)(2,1)S(1)}, u32[]{:S(2)}, u32[]{:S(2)}) async-start(bf16[8,64,1024]{2,1,0:T(8,128)(2,1)} %broadcast_in_dim.17), calls=%async_computation.6 | async-start | bytes 2097152 | tf_op jit(solution)/shard_map/all_to_all | solution.py:62
  173.1 90.7 %reduce-scatter.2.cloned.1.call-start = ((), (), s32[]{:S(2)}) async-start(), calls=%async_computation.8 | async-start | bytes 2162688 | tf_op jit(solution)/shard_map/reduce_scatter | solution.py:90
  175.2 24.2 %copy-start.18 = (pred[64,8,4,256]{3,1,2,0:T(8,128)(4,1)S(1)}, pred[64,8,4,256]{3,1,2,0:T(8,128)(4,1)}, u32[]{:S(2)}) copy-start(pred[64,8,4,256]{3,1,2,0:T(8,128)(4,1)} %copy.27) | copy-start | bytes 1572868
  199.4 2.4 copy-start.2
  199.4 2.4 copy-start.1
  199.4 2.4 copy-start.6
  203.8 34.9 %all-to-all-start.6 = ((f32[32,16,1024]{2,1,0:T(8,128)}), f32[32,16,1024]{2,1,0:T(8,128)S(1)}, u32[]{:S(2)}, u32[]{:S(2)}) async-start(f32[32,16,1024]{2,1,0:T(8,128)} %bitcast.9), calls=%async_computation.7 | async-start | bytes 4194304 | tf_op jit(solution)/shard_map/all_to_all | solution.py:56
  208.9 3.5 %copy-start.3 = (bf16[8,64,1024]{2,1,0:T(8,128)(2,1)S(1)}, bf16[8,64,1024]{2,1,0:T(8,128)(2,1)}, u32[]{:S(2)}) copy-start(bf16[8,64,1024]{2,1,0:T(8,128)(2,1)} %copy-done.2) | copy-start | bytes 3145732
  209.0 3.5 %copy-start.12 = (bf16[32,16,1024]{2,1,0:T(8,128)(2,1)S(1)}, bf16[32,16,1024]{2,1,0:T(8,128)(2,1)}, u32[]{:S(2)}) copy-start(bf16[32,16,1024]{2,1,0:T(8,128)(2,1)} %copy-done.10) | copy-start | bytes 3145732
  209.0 3.5 %copy-start.19 = (pred[64,8,4,256]{3,1,2,0:T(8,128)(4,1)S(1)}, pred[64,8,4,256]{3,1,2,0:T(8,128)(4,1)}, u32[]{:S(2)}) copy-start(pred[64,8,4,256]{3,1,2,0:T(8,128)(4,1)} %copy.27) | copy-start | bytes 1572868
  214.5 3.0 %copy-start.4 = (bf16[8,64,1024]{2,1,0:T(8,128)(2,1)S(1)}, bf16[8,64,1024]{2,1,0:T(8,128)(2,1)}, u32[]{:S(2)}) copy-start(bf16[8,64,1024]{2,1,0:T(8,128)(2,1)} %copy-done.2) | copy-start | bytes 3145732
Sparse Core Ops, SparseCore 0:
  177.7 86.0 reduce-scatter.1
